TPU v7x, 128 devices: a whole 4x4x4 slice. The times are simulated.
128 devices in a mesh: row: 16 (over y_lo, x, core), col: 8 (over z, y_hi).
Axes of the slice: x: 4, y: 4 (y_hi: 2, y_lo: 2; y = y_hi * 2 + y_lo), z: 4, core: 2. Of those that a mesh axis runs over, the one named last changes fastest.
Arguments:
- gate_feats: bfloat16 [16, 8, 1024, 256], P('row', 'col'), may hold values from -6 to 6
- adjacency: int32 [16, 8, 8, 5, 128, 128], P('row', 'col'), may hold values 0 or 1
- gate_count: int32 [16, 8], P('row', 'col'), may hold values from 128 to 1024, as said below
- membership: int32 [16, 8, 512, 1024], P('row', 'col'), may hold values 0 or 1
- tok_count: int32 [16, 8], P('row', 'col'), may hold values from 64 to 512, as said below
- w_msg: bfloat16 [256, 256], replicated, may hold values from -0.375 to 0.375
- w_query: bfloat16 [256, 256], replicated, may hold values from -0.375 to 0.375
- w_key: bfloat16 [256, 256], replicated, may hold values from -0.375 to 0.375
- w_value: bfloat16 [256, 256], replicated, may hold values from -0.375 to 0.375
- w_out: bfloat16 [256, 256], replicated, may hold values from -0.375 to 0.375
- w_score: bfloat16 [256], replicated, may hold values from -0.375 to 0.375
- cotangent: float32 [16, 8, 512], P('row', 'col'), may hold values from -6 to 6
Outputs:
- value_out: float32 [16, 8, 512], P('row', 'col')
- g_msg: float32 [256, 256], replicated
- g_query: float32 [256, 256], replicated
- g_key: float32 [256, 256], replicated
- g_value: float32 [256, 256], replicated
- g_out: float32 [256, 256], replicated
- g_score: float32 [256], replicated
Inputs may be any that keep to these rules, and one draw needn't show every extreme that they name: `gate_count`: some tile is full in every draw. `tok_count`: some tile is full in every draw.
All inputs are finite; a program needn't handle non-finite values. No bound on the sum of `adjacency` or of `membership` on one device may be relied on, other than what follows from the above.
Results may differ from a plain program's by a relative error of at most 0.017.
Values may be sent and summed in bfloat16 or wider, within the bound.
No kernel may reach another device: no remote copies, remote signals or barrier semaphores. Data moves between devices by JAX's collectives and lax.ppermute only.
A program may use at most 128 MiB of HBM per device.

v0:
```python
import math

import jax
import jax.numpy as jnp
from jax import lax
from jax.sharding import PartitionSpec as P

H = 256
HEADS = 2
HD = 128
BLK = 128
NB = 8
NT = 512


EPS = 1e-06


def with_halo(array, sides, width):
    for axis, dim in sides:
        size, length = (lax.axis_size(axis), array.shape[dim])
        up = [(i, (i + 1) % size) for i in range(size - 1)]
        down = [(j, i) for i, j in up]
        last = lax.slice_in_dim(array, length - width, length, axis=dim)
        first = lax.slice_in_dim(array, 0, width, axis=dim)
        before = lax.ppermute(last, axis, up)
        after = lax.ppermute(first, axis, down)
        array = jnp.concatenate([before, array, after], axis=dim)
    return array


def silu_grad(preact):
    sigmoid_val = jax.nn.sigmoid(preact)
    return sigmoid_val * (1.0 + preact * (1.0 - sigmoid_val))


def rms_forward(values_in):
    rscale = lax.rsqrt(jnp.mean(values_in * values_in, axis=-1, keepdims=True) + EPS)
    return (values_in * rscale, rscale)


def rms_backward(grad_in, normed, rscale):
    return rscale * (grad_in - normed * jnp.mean(grad_in * normed, axis=-1, keepdims=True))


def split_heads(rows_in):
    return rows_in.reshape(rows_in.shape[0], HEADS, HD)


def score_probs(query_rows, key_rows):
    scores = jnp.einsum(
        "qhd,khd->hqk",
        split_heads(query_rows),
        split_heads(key_rows),
        preferred_element_type=jnp.float32,
    )
    return jax.nn.sigmoid(scores / math.sqrt(HD) - math.log(NT))


def attend_sum(query_rows, key_rows, value_rows):
    weights = score_probs(query_rows, key_rows).astype(jnp.bfloat16)
    output = jnp.einsum(
        "hqk,khd->qhd", weights, split_heads(value_rows), preferred_element_type=jnp.float32
    )
    return output.reshape(query_rows.shape[0], H)


def score_grads(query_rows, grad_rows, key_rows, value_rows):
    probs_val = score_probs(query_rows, key_rows)
    grad_prob = jnp.einsum(
        "qhd,khd->hqk",
        split_heads(grad_rows),
        split_heads(value_rows),
        preferred_element_type=jnp.float32,
    )
    grad_score = (grad_prob * probs_val * (1.0 - probs_val) / math.sqrt(HD)).astype(jnp.bfloat16)
    return (probs_val.astype(jnp.bfloat16), grad_score)


def query_grad(query_rows, grad_rows, key_rows, value_rows):
    weights, grad_score = score_grads(query_rows, grad_rows, key_rows, value_rows)
    grad_query = jnp.einsum(
        "hqk,khd->qhd", grad_score, split_heads(key_rows), preferred_element_type=jnp.float32
    )
    return grad_query.reshape(query_rows.shape[0], H)


def key_value_grads(query_rows, grad_rows, key_rows, value_rows):
    weights, grad_score = score_grads(query_rows, grad_rows, key_rows, value_rows)
    grad_key = jnp.einsum(
        "hqk,qhd->khd", grad_score, split_heads(query_rows), preferred_element_type=jnp.float32
    )
    grad_val = jnp.einsum(
        "hqk,qhd->khd", weights, split_heads(grad_rows), preferred_element_type=jnp.float32
    )
    return jnp.concatenate(
        [grad_key.reshape(key_rows.shape[0], H), grad_val.reshape(key_rows.shape[0], H)], axis=1
    )


def project(rows_in, weight_mat):
    return jnp.dot(rows_in, weight_mat, preferred_element_type=jnp.float32).astype(jnp.bfloat16)


def body(
    gate_feats,
    adjacency,
    gate_count,
    membership,
    tok_count,
    w_msg,
    w_query,
    w_key,
    w_value,
    w_out,
    w_score,
    cotangent,
):
    gate_total = gate_feats.shape[2]
    gate_live = (jnp.arange(gate_total) < gate_count[0, 0]).astype(jnp.float32)
    live_feats = (gate_feats[0, 0].astype(jnp.float32) * gate_live[:, None]).astype(jnp.bfloat16)
    padded = with_halo(live_feats[None, None], (("row", 0), ("col", 1)), 1)
    sources = jnp.stack(
        [padded[1, 1], padded[0, 1], padded[2, 1], padded[1, 0], padded[1, 2]], axis=0
    )
    sources = sources.reshape(5, NB, BLK, H)
    adj_tiles = adjacency[0, 0]
    aggregate = jnp.einsum(
        "bkij,kbjh->bih",
        adj_tiles.astype(jnp.bfloat16),
        sources,
        preferred_element_type=jnp.float32,
    )
    degree = jnp.sum(adj_tiles, axis=(1, 3)).astype(jnp.float32)
    message = (aggregate / (degree[:, :, None] + 1.0)).astype(jnp.bfloat16).reshape(gate_total, H)
    preact = jnp.dot(message, w_msg, preferred_element_type=jnp.float32)
    hidden = (gate_live[:, None] * (live_feats.astype(jnp.float32) + jax.nn.silu(preact))).astype(
        jnp.bfloat16
    )
    member_rows = membership[0, 0].astype(jnp.bfloat16)
    member_count = jnp.sum(membership[0, 0], axis=1).astype(jnp.float32)[:, None]
    pooled = jnp.dot(member_rows, hidden, preferred_element_type=jnp.float32) / (member_count + 1.0)
    normed, rscale = rms_forward(pooled)
    token_live = (jnp.arange(NT) < tok_count[0, 0]).astype(jnp.float32)[:, None]
    tokens = (token_live * normed).astype(jnp.bfloat16)
    query_own = project(tokens, w_query)
    zero_rows = jnp.zeros((NT, H), jnp.float32)
    key_own = project(tokens, w_key)
    value_own = project(tokens, w_value)
    attended = attend_sum(
        query_own,
        lax.all_gather(key_own, "col", axis=0, tiled=True),
        lax.all_gather(value_own, "col", axis=0, tiled=True),
    )
    attended = attended.astype(jnp.bfloat16)
    proj = jnp.dot(attended, w_out, preferred_element_type=jnp.float32)
    pnormed, pscale = rms_forward(proj)
    mixed = tokens.astype(jnp.float32) + pnormed
    score_w = w_score.astype(jnp.float32)
    value_out = token_live[:, 0] * jnp.sum(mixed * score_w, axis=1)
    loss_weight = 1.0 / math.sqrt(lax.axis_size("row") * lax.axis_size("col") * NT)
    grad_value = token_live[:, 0] * cotangent[0, 0] * loss_weight
    g_score = jnp.sum(mixed * grad_value[:, None], axis=0)
    grad_mixed = grad_value[:, None] * score_w
    grad_proj = rms_backward(grad_mixed, pnormed, pscale).astype(jnp.bfloat16)
    g_out = jnp.einsum("nh,ne->he", attended, grad_proj, preferred_element_type=jnp.float32)
    grad_attn = jnp.dot(grad_proj, w_out.T, preferred_element_type=jnp.float32).astype(jnp.bfloat16)
    key_all, value_all = (
        lax.all_gather(key_own, "col", axis=0, tiled=True),
        lax.all_gather(value_own, "col", axis=0, tiled=True),
    )

    def add_query(running, pair_in):
        return (running + query_grad(query_own, grad_attn, pair_in[0], pair_in[1]), 0)

    grad_query, unused = lax.scan(
        add_query, zero_rows, (key_all.reshape(-1, NT, H), value_all.reshape(-1, NT, H))
    )
    key_part = key_all.reshape(lax.axis_size("col") * NT // NT, NT, H)
    value_part = value_all.reshape(lax.axis_size("col") * NT // NT, NT, H)
    terms = lax.map(
        lambda pair_in: key_value_grads(query_own, grad_attn, pair_in[0], pair_in[1]),
        (key_part, value_part),
    )
    key_sums = lax.psum_scatter(
        terms.reshape(lax.axis_size("col") * NT, 2 * H), "col", scatter_dimension=0, tiled=True
    )
    grad_query = grad_query.astype(jnp.bfloat16)
    grad_key = key_sums[:, :H].astype(jnp.bfloat16)
    grad_val = key_sums[:, H:].astype(jnp.bfloat16)
    g_query = jnp.einsum("nh,ne->he", tokens, grad_query, preferred_element_type=jnp.float32)
    g_key = jnp.einsum("nh,ne->he", tokens, grad_key, preferred_element_type=jnp.float32)
    g_value = jnp.einsum("nh,ne->he", tokens, grad_val, preferred_element_type=jnp.float32)
    grad_tokens = grad_mixed + jnp.dot(grad_query, w_query.T, preferred_element_type=jnp.float32)
    grad_tokens = grad_tokens + jnp.dot(grad_key, w_key.T, preferred_element_type=jnp.float32)
    grad_tokens = grad_tokens + jnp.dot(grad_val, w_value.T, preferred_element_type=jnp.float32)
    grad_pooled = rms_backward(token_live * grad_tokens, normed, rscale)
    grad_scaled = (grad_pooled / (member_count + 1.0)).astype(jnp.bfloat16)
    grad_hidden = jnp.einsum(
        "ng,nh->gh", member_rows, grad_scaled, preferred_element_type=jnp.float32
    )
    grad_pre = (gate_live[:, None] * grad_hidden * silu_grad(preact)).astype(jnp.bfloat16)
    g_msg = jnp.einsum("gh,ge->he", message, grad_pre, preferred_element_type=jnp.float32)
    summed = lax.psum((g_msg, g_query, g_key, g_value, g_out, g_score), ("row", "col"))
    return (value_out[None, None], summed[0], summed[1], summed[2], summed[3], summed[4], summed[5])


def solution(mesh):
    placed = (
        P("row", "col", None, None),
        P("row", "col", None, None, None, None),
        P("row", "col"),
        P("row", "col", None, None),
        P("row", "col"),
        P(),
        P(),
        P(),
        P(),
        P(),
        P(),
        P("row", "col", None),
    )
    return jax.shard_map(
        body,
        mesh=mesh,
        in_specs=placed,
        out_specs=(P("row", "col", None), P(), P(), P(), P(), P(), P()),
        check_vma=False,
    )
```

profile of v0, /device:TPU:0, one launch (start us, length us, event | category | flops | bytes accessed | tf_op | source)
XLA Modules:
  0.0 573.0 jit_solution(18341425830394711041)
XLA Ops:
  12.2 4.1 collective-permute-done.1
  17.6 6.4 %collective-permute-start.2 = (bf16[3,1,1024,256]{3,2,1,0:T(8,128)(2,1)}, bf16[3,1,1024,256]{3,2,1,0:T(8,128)(2,1)}, u32[]{:S(2)}, u32[]{:S(2)}) collective-permute-start(bf16[3,1,1024,256]{3,2,1,0:T(8,128)(2,1)} %pad_maximum_fusion), channel_id=1, source_target_pairs={{0,1},{1,2},{2,3},{3,4},{4,5},{5,6},{6,7},{8,9},{9,10},{10,11},{11... | collective-permute-start | bytes 4718600 | tf_op jit(solution)/shard_map/ppermute | solution.py:26
  25.5 1.8 reduce_sum.75
  29.4 22.2 %collective-permute-done.2 = bf16[3,1,1024,256]{3,2,1,0:T(8,128)(2,1)} collective-permute-done((bf16[3,1,1024,256]{3,2,1,0:T(8,128)(2,1)}, bf16[3,1,1024,256]{3,2,1,0:T(8,128)(2,1)}, u32[]{:S(2)}, u32[]{:S(2)}) %collective-permute-start.2) | collective-permute-done | bytes 1572896 | tf_op jit(solution)/shard_map/ppermute | solution.py:26
  52.7 34.7 %collective-permute-done.3 = bf16[3,1,1024,256]{3,2,1,0:T(8,128)(2,1)} collective-permute-done((bf16[3,1,1024,256]{3,2,1,0:T(8,128)(2,1)}, bf16[3,1,1024,256]{3,2,1,0:T(8,128)(2,1)}, u32[]{:S(2)}, u32[]{:S(2)}) %collective-permute-start.3) | collective-permute-done | bytes 1572896 | tf_op jit(solution)/shard_map/ppermute | solution.py:27
  94.8 65.4 %all-gather.3.cloned.1.call-done = bf16[4096,256]{1,0:T(8,128)(2,1)} async-done(((bf16[512,256]{1,0:T(8,128)(2,1)}), bf16[4096,256]{1,0:T(8,128)(2,1)}) %all-gather.3.cloned.1.call-update) | async-done | bytes 2097168 | tf_op jit(solution)/shard_map/all_gather | solution.py:153
  160.2 2.9 copy.43
  163.1 51.9 %all-gather.5.cloned.1.call-done = bf16[4096,256]{1,0:T(8,128)(2,1)} async-done(((bf16[512,256]{1,0:T(8,128)(2,1)}), bf16[4096,256]{1,0:T(8,128)(2,1)}) %all-gather.5.cloned.1.call-update) | async-done | bytes 2097168 | tf_op jit(solution)/shard_map/all_gather | solution.py:152
  215.0 4.2 copy.44
  219.2 9.6 %fusion.32 = bf16[2,128,512]{2,1,0:T(8,128)(2,1)} fusion(bf16[4096,2,128]{0,2,1:T(8,128)(2,1)S(1)} %bitcast.190, bf16[512,2,128]{0,2,1:T(8,128)(2,1)S(1)} %bitcast.182, bf16[4096,2,128]{0,2,1:T(8,128)(2,1)} %bitcast.191), kind=kOutput, calls=%fused_computation.49 | convolution fusion | flops 2172780544 | bytes 4718592 | tf_op jit(solution)/shard_map/hqk,khd->qhd/dot_general | solution.py:62
  232.4 1.8 convolution_convert_fusion
  235.2 2.4 copy.30
  237.7 52.7 %while.25 = (s32[]{:T(128)}, f32[8,512,512]{2,1,0:T(8,128)}, bf16[8,512,256]{2,1,0:T(8,128)(2,1)}, bf16[512,256]{0,1:T(8,128)(2,1)S(1)}, bf16[8,512,256]{1,2,0:T...) while((s32[]{:T(128)}, f32[8,512,512]{2,1,0:T(8,128)}, bf16[8,512,256]{2,1,0:T(8,128)(2,1)}, ...), condition=%wide.region_9.10_spmd, body=%wide.region_8.9_spmd.sunk | while | flops 542900224 | bytes 18875020 | solution.py:181
  240.6 1.7 fusion.152
  253.7 1.7 fusion.152
  280.0 1.7 fusion.152
  291.5 53.9 %while.26 = (s32[]{:T(128)}, f32[512,256]{0,1:T(8,128)S(1)}, bf16[8,512,256]{1,2,0:T(8,128)(2,1)}, bf16[8,512,256]{2,1,0:T(8,128)(2,1)}, bf16[512,256]{1,0:T(8,1...) while((s32[]{:T(128)}, f32[512,256]{0,1:T(8,128)S(1)}, ...), condition=%wide.region_7.8_spmd.clone, body=%wide.region_6.7_spmd.clone.sunk | while | flops 408158208 | bytes 9437287 | solution.py:176
  295.7 2.3 fusion.160
  302.4 2.3 fusion.160
  309.1 2.3 fusion.160
  315.9 2.3 fusion.160
  320.9 1.7 constant_dynamic-slice_fusion.10
  322.6 2.4 fusion.160
  329.4 2.3 fusion.160
  336.2 2.3 fusion.160
  342.9 2.3 fusion.160
  346.4 2.1 fusion.91
  348.5 54.1 %reduce-scatter.2.cloned.1.call-done = f32[512,512]{1,0:T(8,128)} async-done(((f32[4096,512]{1,0:T(8,128)}), f32[512,512]{1,0:T(8,128)}) %reduce-scatter.2.cloned.1.call-update) | async-done | bytes 1048592 | tf_op jit(solution)/shard_map/reduce_scatter | solution.py:185
  408.6 3.2 fusion.28
  411.8 64.3 %psum.47 = f32[256]{0:T(256)} all-reduce(f32[256]{0:T(256)S(1)} %copy-done.29), channel_id=1, replica_groups=mesh['row'=16,'col'=8] {'row','col'}, use_global_device_ids=true, to_apply=%region_18.19 | all-reduce | flops 256 | bytes 2048 | tf_op jit(solution)/shard_map/psum | solution.py:204
  476.7 82.3 %all-reduce.3.cloned.1.call-done = (f32[256,256]{1,0:T(8,128)}, f32[256,256]{1,0:T(8,128)}, f32[256,256]{1,0:T(8,128)}, f32[256,256]{1,0:T(8,128)}, f32[256,256]{1,0:T(8,128)}) async-done(((f32[256,256]{1,0:T(8,128)}, f32[256,256]{1,0:T(8,128)}, f32[256,256]{1,0:T(8,128)}, f32[256,256]{1,0:T(8,128)}, f32[256,256]{1,0:T(8,128)}), (f32[256,256]{1,0:T(8,128)}, f32[256,256]{1,0:T(8,128)}, f32[256,256]{1,0:T(8,128)}, ...) | async-done | bytes 1310736 | tf_op jit(solution)/shard_map/psum | solution.py:204
  559.1 1.7 copy.99
  (270 shorter events, 116.2 us)
Async XLA Ops:
  7.2 221.6 %copy-start = (bf16[256,256]{1,0:T(8,128)(2,1)S(1)}, bf16[256,256]{1,0:T(8,128)(2,1)}, u32[]{:S(2)}) copy-start(bf16[256,256]{1,0:T(8,128)(2,1)} %param.25) | copy-start | bytes 393220
  7.2 153.0 %all-gather.3.cloned.1.call-start = ((), (), s32[]{:S(2)}) async-start(), calls=%async_computation.1 | async-start | bytes 2359296 | tf_op jit(solution)/shard_map/all_gather | solution.py:153
  7.9 81.9 %copy-start.24 = (f32[1024]{0:T(1024)}, f32[1024]{0:T(1024)S(1)}, u32[]{:S(2)}) copy-start(f32[1024]{0:T(1024)S(1)} %fusion.84) | copy-start | bytes 12292
  7.9 17.4 %copy-start.7 = (s32[1,1,8,5,128,128]{5,4,3,2,1,0:T(8,128)S(1)}, s32[1,1,8,5,128,128]{5,4,3,2,1,0:T(8,128)}, u32[]{:S(2)}) copy-start(s32[1,1,8,5,128,128]{5,4,3,2,1,0:T(8,128)} %param.17) | copy-start | bytes 7864324
  9.3 2.8 collective-permute-start
  10.7 5.6 collective-permute-start.1
  12.2 4.1 copy-start.12
  17.6 10.5 %copy-start.10 = (bf16[1,1,1024,256]{3,2,1,0:T(8,128)(2,1)S(1)}, bf16[1,1,1024,256]{3,2,1,0:T(8,128)(2,1)}, u32[]{:S(2)}) copy-start(bf16[1,1,1024,256]{3,2,1,0:T(8,128)(2,1)} %param.16) | copy-start | bytes 1572868
  17.6 34.0 %collective-permute-start.2 = (bf16[3,1,1024,256]{3,2,1,0:T(8,128)(2,1)}, bf16[3,1,1024,256]{3,2,1,0:T(8,128)(2,1)}, u32[]{:S(2)}, u32[]{:S(2)}) collective-permute-start(bf16[3,1,1024,256]{3,2,1,0:T(8,128)(2,1)} %pad_maximum_fusion), channel_id=1, source_target_pairs={{0,1},{1,2},{2,3},{3,4},{4,5},{5,6},{6,7},{8,9},{9,10},{10,11},{11... | collective-permute-start | bytes 4718600 | tf_op jit(solution)/shard_map/ppermute | solution.py:26
  24.0 63.5 %collective-permute-start.3 = (bf16[3,1,1024,256]{3,2,1,0:T(8,128)(2,1)}, bf16[3,1,1024,256]{3,2,1,0:T(8,128)(2,1)}, u32[]{:S(2)}, u32[]{:S(2)}) collective-permute-start(bf16[3,1,1024,256]{3,2,1,0:T(8,128)(2,1)} %pad_maximum_fusion), channel_id=1, source_target_pairs={{1,0},{2,1},{3,2},{4,3},{5,4},{6,5},{7,6},{9,8},{10,9},{11,10},{12... | collective-permute-start | bytes 4718600 | tf_op jit(solution)/shard_map/ppermute | solution.py:27
  27.3 2.1 copy-start.14
  28.0 61.8 %copy-start.31 = (f32[512]{0:T(512)}, f32[512]{0:T(512)S(1)}, u32[]{:S(2)}) copy-start(f32[512]{0:T(512)S(1)} %convert_add_fusion.2) | copy-start | bytes 6148
  89.3 2.1 copy-start.21
  90.5 2.2 copy-start.17
  91.5 138.7 %copy-start.4 = (f32[256,512]{1,0:T(8,128)}, f32[256,512]{1,0:T(8,128)S(1)}, u32[]{:S(2)}) copy-start(f32[256,512]{1,0:T(8,128)S(1)} %get-tuple-element.241) | copy-start | bytes 1572868
  91.5 2.4 copy-start.33
  91.5 3.0 copy-start.30
  91.6 3.0 copy-start.19
  92.6 122.4 %all-gather.5.cloned.1.call-start = ((), (), s32[]{:S(2)}) async-start(), calls=%async_computation.2 | async-start | bytes 2359296 | tf_op jit(solution)/shard_map/all_gather | solution.py:152
  93.7 308.9 %reduce-scatter.2.cloned.1.call-start = ((), (), s32[]{:S(2)}) async-start(), calls=%async_computation.3 | async-start | bytes 9437184 | tf_op jit(solution)/shard_map/reduce_scatter | solution.py:185
  228.8 6.4 %copy-start.3 = (bf16[4096,256]{1,0:T(8,128)(2,1)S(1)}, bf16[4096,256]{1,0:T(8,128)(2,1)}, u32[]{:S(2)}) copy-start(bf16[4096,256]{1,0:T(8,128)(2,1)} %all-gather.5.cloned.1.call-done) | copy-start | bytes 6291460
  290.4 268.7 %all-reduce.3.cloned.1.call-start = ((), (), s32[]{:S(2)}) async-start(), calls=%async_computation.4 | async-start | bytes 2621440 | tf_op jit(solution)/shard_map/psum | solution.py:204
  348.5 58.9 %copy-start.5 = (f32[256,512]{1,0:T(8,128)S(1)}, f32[256,512]{1,0:T(8,128)}, u32[]{:S(2)}) copy-start(f32[256,512]{1,0:T(8,128)} %copy-done.4) | copy-start | bytes 1572868
  348.5 58.9 %copy-start.26 = (f32[256]{0:T(256)S(1)}, f32[256]{0:T(256)}, u32[]{:S(2)}) copy-start(f32[256]{0:T(256)} %convert_element_type.188) | copy-start | bytes 3076
  402.6 4.5 copy-start.18
  402.6 4.8 copy-start.20
  405.8 2.7 copy-start.9
  405.8 2.7 copy-start.25
  405.8 2.7 copy-start.32
  408.6 3.3 copy-start.29
  408.6 67.6 %copy-start.27 = (f32[512]{0:T(512)S(1)}, f32[512]{0:T(512)}, u32[]{:S(2)}) copy-start(f32[512]{0:T(512)} %get-tuple-element.209) | copy-start | bytes 6148
  559.1 6.7 %copy-start.22 = (f32[256,256]{1,0:T(8,128)S(1)}, f32[256,256]{1,0:T(8,128)}, u32[]{:S(2)}) copy-start(f32[256,256]{1,0:T(8,128)} %get-tuple-element.370) | copy-start | bytes 786436
  (24 other events, 36.2 us)
Sparse Core Ops, SparseCore 0:
  92.8 67.3 all-gather.2
  163.1 51.8 all-gather.4
  290.5 112.0 reduce-scatter.1
  411.9 147.0 all-reduce.2
where the time goes:
time: 577 us; the launch traced here: 573 us
  waiting for transfers between devices  315 us (55%)
  local copies, waits for them, and re-layouts  82.6 us (14%)
  matrix products  72.8 us (13%)
  blocking collectives  64.3 us (11%)
  between operations  15.6 us (3%)
  other arithmetic  10.9 us (2%)
  starting transfers between devices  10.8 us (2%)
    psum x1, waiting for transfers between devices, body(): lax.psum((g_msg, g_query, g_key, g_value, g_out, g_score), ('row', 'col'))  82.3 us
    all_gather x1, waiting for transfers between devices, body(): lax.all_gather(value_own, 'col', axis=0, tiled=True)  65.4 us
    psum x1, blocking collectives, body(): lax.psum((g_msg, g_query, g_key, g_value, g_out, g_score), ('row', 'col'))  64.3 us
    reduce_scatter x1, waiting for transfers between devices, body(): lax.psum_scatter(terms.reshape(lax.axis_size('col') * NT, 2 * H), 'col',...  54.1 us
    all_gather x1, waiting for transfers between devices, body(): lax.all_gather(key_own, 'col', axis=0, tiled=True)  51.9 us
    ppermute x2, waiting for transfers between devices, with_halo(): after = lax.ppermute(first, axis, down)  38.8 us
    dynamic_slice x32, local copies, waits for them, and re-layouts, body(): lax.scan(add_query, zero_rows, (key_all.reshape(-1, NT, H), value_all.res...  37.6 us
    ppermute x2, waiting for transfers between devices, with_halo(): before = lax.ppermute(last, axis, up)  22.4 us
  transfers between devices with their start and end apart: 8, of which 8 were waited for; matrix products, arithmetic and copies ran while one was open for 12% of the time, Pallas kernels for 0%

commit v1 on v0

--- a/solution.py
+++ b/solution.py
@@ -29,6 +29,40 @@
     return array
 
 
+def gather_shifted(rows_in, axis):
+    size = lax.axis_size(axis)
+    parts = [rows_in]
+    for shift in range(1, size):
+        parts.append(lax.ppermute(rows_in, axis, [(i, (i + shift) % size) for i in range(size)]))
+    return jnp.stack(parts)
+
+
+def reduce_scatter_direct(flat, axis):
+    size = lax.axis_size(axis)
+    own = lax.axis_index(axis)
+    chunks = flat.reshape(size, -1)
+    total = lax.dynamic_index_in_dim(chunks, own, 0, keepdims=False)
+    for shift in range(1, size):
+        piece = lax.dynamic_index_in_dim(chunks, (own + shift) % size, 0, keepdims=False)
+        total = total + lax.ppermute(piece, axis, [(i, (i + shift) % size) for i in range(size)])
+    return total
+
+
+def all_gather_direct(chunk, axis):
+    size = lax.axis_size(axis)
+    own = lax.axis_index(axis)
+    stacked = gather_shifted(chunk, axis)
+    order = (own - jnp.arange(size)) % size
+    return jnp.take(stacked, order, axis=0).reshape(-1)
+
+
+def all_reduce_direct(flat):
+    part = reduce_scatter_direct(flat, "col")
+    part = reduce_scatter_direct(part, "row")
+    part = all_gather_direct(part, "row")
+    return all_gather_direct(part, "col")
+
+
 def silu_grad(preact):
     sigmoid_val = jax.nn.sigmoid(preact)
     return sigmoid_val * (1.0 + preact * (1.0 - sigmoid_val))
@@ -55,47 +89,6 @@
         preferred_element_type=jnp.float32,
     )
     return jax.nn.sigmoid(scores / math.sqrt(HD) - math.log(NT))
-
-
-def attend_sum(query_rows, key_rows, value_rows):
-    weights = score_probs(query_rows, key_rows).astype(jnp.bfloat16)
-    output = jnp.einsum(
-        "hqk,khd->qhd", weights, split_heads(value_rows), preferred_element_type=jnp.float32
-    )
-    return output.reshape(query_rows.shape[0], H)
-
-
-def score_grads(query_rows, grad_rows, key_rows, value_rows):
-    probs_val = score_probs(query_rows, key_rows)
-    grad_prob = jnp.einsum(
-        "qhd,khd->hqk",
-        split_heads(grad_rows),
-        split_heads(value_rows),
-        preferred_element_type=jnp.float32,
-    )
-    grad_score = (grad_prob * probs_val * (1.0 - probs_val) / math.sqrt(HD)).astype(jnp.bfloat16)
-    return (probs_val.astype(jnp.bfloat16), grad_score)
-
-
-def query_grad(query_rows, grad_rows, key_rows, value_rows):
-    weights, grad_score = score_grads(query_rows, grad_rows, key_rows, value_rows)
-    grad_query = jnp.einsum(
-        "hqk,khd->qhd", grad_score, split_heads(key_rows), preferred_element_type=jnp.float32
-    )
-    return grad_query.reshape(query_rows.shape[0], H)
-
-
-def key_value_grads(query_rows, grad_rows, key_rows, value_rows):
-    weights, grad_score = score_grads(query_rows, grad_rows, key_rows, value_rows)
-    grad_key = jnp.einsum(
-        "hqk,qhd->khd", grad_score, split_heads(query_rows), preferred_element_type=jnp.float32
-    )
-    grad_val = jnp.einsum(
-        "hqk,qhd->khd", weights, split_heads(grad_rows), preferred_element_type=jnp.float32
-    )
-    return jnp.concatenate(
-        [grad_key.reshape(key_rows.shape[0], H), grad_val.reshape(key_rows.shape[0], H)], axis=1
-    )
 
 
 def project(rows_in, weight_mat):
@@ -143,16 +136,21 @@
     normed, rscale = rms_forward(pooled)
     token_live = (jnp.arange(NT) < tok_count[0, 0]).astype(jnp.float32)[:, None]
     tokens = (token_live * normed).astype(jnp.bfloat16)
-    query_own = project(tokens, w_query)
-    zero_rows = jnp.zeros((NT, H), jnp.float32)
-    key_own = project(tokens, w_key)
-    value_own = project(tokens, w_value)
-    attended = attend_sum(
-        query_own,
-        lax.all_gather(key_own, "col", axis=0, tiled=True),
-        lax.all_gather(value_own, "col", axis=0, tiled=True),
-    )
-    attended = attended.astype(jnp.bfloat16)
+
+    tokens_all = gather_shifted(tokens, "col").reshape(-1, H)
+    query_all = project(tokens_all, w_query)
+    key_all = project(tokens_all, w_key)
+    value_all = project(tokens_all, w_value)
+    query_own = query_all[:NT]
+    key_own = key_all[:NT]
+    value_own = value_all[:NT]
+
+    probs_own = score_probs(query_own, key_all)
+    weights_own = probs_own.astype(jnp.bfloat16)
+    attended = jnp.einsum(
+        "hqk,khd->qhd", weights_own, split_heads(value_all), preferred_element_type=jnp.float32
+    )
+    attended = attended.reshape(NT, H).astype(jnp.bfloat16)
     proj = jnp.dot(attended, w_out, preferred_element_type=jnp.float32)
     pnormed, pscale = rms_forward(proj)
     mixed = tokens.astype(jnp.float32) + pnormed
@@ -165,29 +163,32 @@
     grad_proj = rms_backward(grad_mixed, pnormed, pscale).astype(jnp.bfloat16)
     g_out = jnp.einsum("nh,ne->he", attended, grad_proj, preferred_element_type=jnp.float32)
     grad_attn = jnp.dot(grad_proj, w_out.T, preferred_element_type=jnp.float32).astype(jnp.bfloat16)
-    key_all, value_all = (
-        lax.all_gather(key_own, "col", axis=0, tiled=True),
-        lax.all_gather(value_own, "col", axis=0, tiled=True),
-    )
-
-    def add_query(running, pair_in):
-        return (running + query_grad(query_own, grad_attn, pair_in[0], pair_in[1]), 0)
-
-    grad_query, unused = lax.scan(
-        add_query, zero_rows, (key_all.reshape(-1, NT, H), value_all.reshape(-1, NT, H))
-    )
-    key_part = key_all.reshape(lax.axis_size("col") * NT // NT, NT, H)
-    value_part = value_all.reshape(lax.axis_size("col") * NT // NT, NT, H)
-    terms = lax.map(
-        lambda pair_in: key_value_grads(query_own, grad_attn, pair_in[0], pair_in[1]),
-        (key_part, value_part),
-    )
-    key_sums = lax.psum_scatter(
-        terms.reshape(lax.axis_size("col") * NT, 2 * H), "col", scatter_dimension=0, tiled=True
-    )
-    grad_query = grad_query.astype(jnp.bfloat16)
-    grad_key = key_sums[:, :H].astype(jnp.bfloat16)
-    grad_val = key_sums[:, H:].astype(jnp.bfloat16)
+
+    grad_attn_all = gather_shifted(grad_attn, "col").reshape(-1, H)
+
+    grad_prob_q = jnp.einsum(
+        "qhd,khd->hqk", split_heads(grad_attn), split_heads(value_all),
+        preferred_element_type=jnp.float32,
+    )
+    grad_score_q = (grad_prob_q * probs_own * (1.0 - probs_own) / math.sqrt(HD)).astype(jnp.bfloat16)
+    grad_query = jnp.einsum(
+        "hqk,khd->qhd", grad_score_q, split_heads(key_all), preferred_element_type=jnp.float32
+    ).reshape(NT, H).astype(jnp.bfloat16)
+
+    probs_key = score_probs(query_all, key_own)
+    weights_key = probs_key.astype(jnp.bfloat16)
+    grad_prob_k = jnp.einsum(
+        "qhd,khd->hqk", split_heads(grad_attn_all), split_heads(value_own),
+        preferred_element_type=jnp.float32,
+    )
+    grad_score_k = (grad_prob_k * probs_key * (1.0 - probs_key) / math.sqrt(HD)).astype(jnp.bfloat16)
+    grad_key = jnp.einsum(
+        "hqk,qhd->khd", grad_score_k, split_heads(query_all), preferred_element_type=jnp.float32
+    ).reshape(NT, H).astype(jnp.bfloat16)
+    grad_val = jnp.einsum(
+        "hqk,qhd->khd", weights_key, split_heads(grad_attn_all), preferred_element_type=jnp.float32
+    ).reshape(NT, H).astype(jnp.bfloat16)
+
     g_query = jnp.einsum("nh,ne->he", tokens, grad_query, preferred_element_type=jnp.float32)
     g_key = jnp.einsum("nh,ne->he", tokens, grad_key, preferred_element_type=jnp.float32)
     g_value = jnp.einsum("nh,ne->he", tokens, grad_val, preferred_element_type=jnp.float32)
@@ -201,8 +202,17 @@
     )
     grad_pre = (gate_live[:, None] * grad_hidden * silu_grad(preact)).astype(jnp.bfloat16)
     g_msg = jnp.einsum("gh,ge->he", message, grad_pre, preferred_element_type=jnp.float32)
-    summed = lax.psum((g_msg, g_query, g_key, g_value, g_out, g_score), ("row", "col"))
-    return (value_out[None, None], summed[0], summed[1], summed[2], summed[3], summed[4], summed[5])
+
+    flat = jnp.concatenate(
+        [g.reshape(-1) for g in (g_msg, g_query, g_key, g_value, g_out, g_score)]
+    )
+    devices = lax.axis_size("row") * lax.axis_size("col")
+    pad = (-flat.shape[0]) % devices
+    summed = all_reduce_direct(jnp.pad(flat, (0, pad)))
+    sq = H * H
+    outs = [summed[i * sq:(i + 1) * sq].reshape(H, H) for i in range(5)]
+    g_score_sum = summed[5 * sq:5 * sq + H]
+    return (value_out[None, None], *outs, g_score_sum)
 
 
 def solution(mesh):

time: 577 us -> 370 us (0.64)
  waiting for transfers between devices: 315 us -> 120 us
  starting transfers between devices: 10.8 us -> 115 us
  blocking collectives: 64.3 us -> 0 us
  local copies, waits for them, and re-layouts: 82.6 us -> 44.1 us
  between operations: 15.6 us -> 3.5 us
    all_gather x2 -> x0, waiting for transfers between devices: 117 us -> none  [the longest x1 65.4 us: body(): lax.all_gather(value_own, 'col', axis=0, tiled=True)]
    ppermute x0 -> x58, starting transfers between devices: none -> 103 us  [the longest x36 64.8 us: gather_shifted(): lax.ppermute(rows_in, axis, [(i, (i + shift) % size) for i in range(size)])]
    psum x1 -> x0, waiting for transfers between devices: 82.3 us -> none  [body(): lax.psum((g_msg, g_query, g_key, g_value, g_out, g_score), ('row', 'col'))]
    psum x1 -> x0, blocking collectives: 64.3 us -> none  [body(): lax.psum((g_msg, g_query, g_key, g_value, g_out, g_score), ('row', 'col'))]
    reduce_scatter x1 -> x0, waiting for transfers between devices: 54.1 us -> none  [body(): lax.psum_scatter(terms.reshape(lax.axis_size('col') * NT, 2 * H), 'col',...]
    ppermute x0 -> x58, waiting for transfers between devices: none -> 53.1 us  [the longest x36 38.2 us: gather_shifted(): lax.ppermute(rows_in, axis, [(i, (i + shift) % size) for i in range(size)])]
    dynamic_slice x32 -> x2, local copies, waits for them, and re-layouts: 37.6 us -> 4.36 us  [reduce_scatter_direct(): lax.dynamic_index_in_dim(chunks, (own + shift) % size, 0, keepdims=False)]
    another operation x0 -> x30, local copies, waits for them, and re-layouts: none -> 16.7 us  [the longest x29 13.7 us: gather_shifted(): return jnp.stack(parts)]
  transfers between devices with their start and end apart: 8 -> 62, of which waited for: 8 -> 24; matrix products, arithmetic and copies ran while one was open for 12% -> 11% of each run, Pallas kernels for 0% -> 0%
where the time goes in v1:
time: 370 us; the launch traced here: 363 us
  waiting for transfers between devices  120 us (32%)
  starting transfers between devices  115 us (31%)
  matrix products  70.8 us (19%)
  local copies, waits for them, and re-layouts  44.1 us (12%)
  other arithmetic  9.47 us (3%)
    ppermute x36, starting transfers between devices, gather_shifted(): lax.ppermute(rows_in, axis, [(i, (i + shift) % size) for i in range(size)])  64.8 us
    ppermute x36, waiting for transfers between devices, gather_shifted(): lax.ppermute(rows_in, axis, [(i, (i + shift) % size) for i in range(size)])  38.2 us
    ppermute x22, starting transfers between devices, reduce_scatter_direct(): lax.ppermute(piece, axis, [(i, (i + shift) % size) for i in range(size)])  37.8 us
    ppermute x2, waiting for transfers between devices, with_halo(): after = lax.ppermute(first, axis, down)  37.7 us
    ppermute x2, waiting for transfers between devices, with_halo(): before = lax.ppermute(last, axis, up)  29.4 us
    ppermute x22, waiting for transfers between devices, reduce_scatter_direct(): lax.ppermute(piece, axis, [(i, (i + shift) % size) for i in range(size)])  14.9 us
    dot_general x2, matrix products, score_probs(): jnp.einsum('qhd,khd->hqk', split_heads(query_rows), split_heads(key_rows)...  14.6 us
    another operation x29, local copies, waits for them, and re-layouts, gather_shifted(): return jnp.stack(parts)  13.7 us
  transfers between devices with their start and end apart: 62, of which 24 were waited for; matrix products, arithmetic and copies ran while one was open for 11% of the time, Pallas kernels for 0%

profile of v1, /device:TPU:0, one launch (start us, length us, event | category | flops | bytes accessed | tf_op | source)
XLA Modules:
  0.0 363.0 jit_solution(11782078155129124887)
XLA Ops:
  4.2 3.1 collective-permute-start
  10.1 6.3 %collective-permute-start.2 = (bf16[3,1,1024,256]{3,2,1,0:T(8,128)(2,1)}, bf16[3,1,1024,256]{3,2,1,0:T(8,128)(2,1)}, u32[]{:S(2)}, u32[]{:S(2)}) collective-permute-start(bf16[3,1,1024,256]{3,2,1,0:T(8,128)(2,1)} %pad_maximum_fusion), channel_id=1, source_target_pairs={{0,1},{1,2},{2,3},{3,4},{4,5},{5,6},{6,7},{8,9},{9,10},{10,11},{11... | collective-permute-start | bytes 4718600 | tf_op jit(solution)/shard_map/ppermute | solution.py:26
  21.8 28.0 %collective-permute-done.2 = bf16[3,1,1024,256]{3,2,1,0:T(8,128)(2,1)} collective-permute-done((bf16[3,1,1024,256]{3,2,1,0:T(8,128)(2,1)}, bf16[3,1,1024,256]{3,2,1,0:T(8,128)(2,1)}, u32[]{:S(2)}, u32[]{:S(2)}) %collective-permute-start.2) | collective-permute-done | bytes 1572896 | tf_op jit(solution)/shard_map/ppermute | solution.py:26
  50.9 37.7 %collective-permute-done.3 = bf16[3,1,1024,256]{3,2,1,0:T(8,128)(2,1)} collective-permute-done((bf16[3,1,1024,256]{3,2,1,0:T(8,128)(2,1)}, bf16[3,1,1024,256]{3,2,1,0:T(8,128)(2,1)}, u32[]{:S(2)}, u32[]{:S(2)}) %collective-permute-start.3) | collective-permute-done | bytes 1572896 | tf_op jit(solution)/shard_map/ppermute | solution.py:27
  96.1 5.5 %collective-permute-start.10 = (bf16[512,256]{0,1:T(8,128)(2,1)S(1)}, bf16[512,256]{0,1:T(8,128)(2,1)S(1)}, u32[]{:S(2)}, u32[]{:S(2)}) collective-permute-start(bf16[512,256]{0,1:T(8,128)(2,1)S(1)} %get-tuple-element.35), channel_id=1, source_target_pairs={{0,7},{1,0},{2,1},{3,2},{4,3},{5,4},{6,5},{7,6},{8,15},{9,8},{10,9... | collective-permute-start | bytes 786440 | tf_op jit(solution)/shard_map/ppermute | solution.py:36
  103.2 3.1 collective-permute-done.4
  108.4 3.4 collective-permute-start.7
  112.5 8.3 %collective-permute-done.6 = bf16[512,256]{0,1:T(8,128)(2,1)S(1)} collective-permute-done((bf16[512,256]{0,1:T(8,128)(2,1)S(1)}, bf16[512,256]{0,1:T(8,128)(2,1)S(1)}, u32[]{:S(2)}, u32[]{:S(2)}) %collective-permute-start.6) | collective-permute-done | bytes 262176 | tf_op jit(solution)/shard_map/ppermute | solution.py:36
  135.0 5.2 %add_divide_fusion.1 = f32[2,512,4096]{2,1,0:T(8,128)S(1)} fusion(bf16[512,2,128]{0,2,1:T(8,128)(2,1)S(1)} %bitcast.216, bf16[4096,2,128]{0,2,1:T(8,128)(2,1)S(1)} %bitcast.192), kind=kOutput, calls=%fused_computation.5 | convolution fusion | flops 1094713344 | bytes 19136512 | tf_op jit(solution)/shard_map/qhd,khd->hqk/dot_general | solution.py:85
  140.2 6.8 %fusion.13 = bf16[2,128,512]{2,1,0:T(8,128)(2,1)} fusion(bf16[4096,2,128]{0,2,1:T(8,128)(2,1)} %bitcast.188, f32[2,512,4096]{2,1,0:T(8,128)S(1)} %add_divide_fusion.1), kind=kOutput, calls=%fused_computation.29 | convolution fusion | flops 1078067200 | bytes 19136512 | tf_op jit(solution)/shard_map/hqk,khd->qhd/dot_general | solution.py:150
  152.4 5.0 %collective-permute-start.12 = (bf16[512,256]{0,1:T(8,128)(2,1)}, bf16[512,256]{0,1:T(8,128)(2,1)}, u32[]{:S(2)}, u32[]{:S(2)}) collective-permute-start(bf16[512,256]{0,1:T(8,128)(2,1)} %get-tuple-element.46), channel_id=1, source_target_pairs={{0,2},{1,3},{2,4},{3,5},{4,6},{5,7},{6,0},{7,1},{8,10},{9,11},{10,... | collective-permute-start | bytes 786440 | tf_op jit(solution)/shard_map/ppermute | solution.py:36
  158.5 13.0 %fusion.20 = bf16[2,128,512]{2,1,0:T(8,128)(2,1)S(1)} fusion(bf16[4096,2,128]{0,2,1:T(8,128)(2,1)} %bitcast.193, f32[2,512,4096]{2,1,0:T(8,128)} %copy-done.2, bf16[512,2,128]{0,2,1:T(8,128)(2,1)} %bitcast.32, bf16[4096,2,128]{0,2,1:T(8,128)(2,1)S(1)} %bitcast.189), kind=kOutput, calls=%fused_computation.33 | convolution fusion | flops 2168586240 | bytes 21495808 | tf_op jit(solution)/shard_map/hqk,khd->qhd/dot_general | solution.py:174
  172.7 9.4 %add_divide_fusion = f32[2,4096,512]{2,1,0:T(8,128)} fusion(bf16[4096,2,128]{0,2,1:T(8,128)(2,1)} %bitcast.190, bf16[512,2,128]{0,2,1:T(8,128)(2,1)} %bitcast.215), kind=kOutput, calls=%fused_computation.3 | convolution fusion | flops 1094713344 | bytes 19136512 | tf_op jit(solution)/shard_map/qhd,khd->hqk/dot_general | solution.py:85
  183.4 3.2 collective-permute-start.16
  186.6 3.6 collective-permute-start.15
  194.5 5.0 %collective-permute-start.17 = (bf16[512,256]{0,1:T(8,128)(2,1)}, bf16[512,256]{0,1:T(8,128)(2,1)S(1)}, u32[]{:S(2)}, u32[]{:S(2)}) collective-permute-start(bf16[512,256]{0,1:T(8,128)(2,1)} %get-tuple-element.46), channel_id=1, source_target_pairs={{0,7},{1,0},{2,1},{3,2},{4,3},{5,4},{6,5},{7,6},{8,15},{9,8},{10,9... | collective-permute-start | bytes 786440 | tf_op jit(solution)/shard_map/ppermute | solution.py:36
  200.5 6.4 %collective-permute-done.13 = bf16[512,256]{0,1:T(8,128)(2,1)S(1)} collective-permute-done((bf16[512,256]{0,1:T(8,128)(2,1)}, bf16[512,256]{0,1:T(8,128)(2,1)S(1)}, u32[]{:S(2)}, u32[]{:S(2)}) %collective-permute-start.13) | collective-permute-done | bytes 262176 | tf_op jit(solution)/shard_map/ppermute | solution.py:36
  211.6 3.0 reshape_reshape.4
  214.6 7.0 %fusion.16 = bf16[2,128,512]{2,1,0:T(8,128)(2,1)S(1)} fusion(bf16[4096,2,128]{0,2,1:T(8,128)(2,1)S(1)} %reshape_reshape.4, f32[2,4096,512]{2,1,0:T(8,128)} %add_divide_fusion), kind=kOutput, calls=%fused_computation.30 | convolution fusion | flops 1078067200 | bytes 19136512 | tf_op jit(solution)/shard_map/hqk,qhd->khd/dot_general | solution.py:188
  221.7 13.3 %fusion.19 = bf16[2,128,512]{2,1,0:T(8,128)(2,1)} fusion(bf16[4096,2,128]{0,2,1:T(8,128)(2,1)} %bitcast.191, f32[2,4096,512]{2,1,0:T(8,128)} %add_divide_fusion, bf16[4096,2,128]{0,2,1:T(8,128)(2,1)S(1)} %reshape_reshape.4, bf16[512,2,128]{0,2,1:T(8,128)(2,1)} %bitcast.214), kind=kOutput, calls=%fused_computation.32 | convolution fusion | flops 2168586240 | bytes 21495808 | tf_op jit(solution)/shard_map/hqk,qhd->khd/dot_general | solution.py:185
  243.2 3.8 %dynamic-slice_reduce_fusion.6 = (f32[40992]{0:T(1024)S(1)}, f32[40992]{0:T(1024)S(1)}, f32[40992]{0:T(1024)S(1)}, f32[40992]{0:T(1024)S(1)}, f32[40992]{0:T(102...) fusion(f32[8,40992]{1,0:T(8,128)S(1)} %reshape.364, s32[]{:T(128)S(6)} %select_n.271, ...), kind=kLoop, calls=%fused_computation.107 | loop fusion | bytes 2623520 | tf_op jit(solution)/shard_map/jit(dynamic_index_in_dim)/dynamic_slice | solution.py:46
  249.4 3.3 collective-permute-start.24
  256.1 3.4 collective-permute-start.21
  261.0 4.2 %collective-permute-done.23 = f32[40992]{0:T(1024)S(1)} collective-permute-done((f32[40992]{0:T(1024)S(1)}, f32[40992]{0:T(1024)S(1)}, u32[]{:S(2)}, u32[]{:S(2)}) %collective-permute-start.23) | collective-permute-done | bytes 164000 | tf_op jit(solution)/shard_map/ppermute | solution.py:47
  270.4 3.8 %collective-permute-start.39 = (f32[2562]{0:T(1024)S(1)}, f32[2562]{0:T(1024)S(1)}, u32[]{:S(2)}, u32[]{:S(2)}) collective-permute-start(f32[2562]{0:T(1024)S(1)} %get-tuple-element.19), channel_id=1, source_target_pairs={{0,120},{8,0},{16,8},{24,16},{32,24},{40,32},{48,40},{56,48},{64,5... | collective-permute-start | bytes 30752 | tf_op jit(solution)/shard_map/ppermute | solution.py:47
  274.7 8.4 %collective-permute-start.36 = (f32[2562]{0:T(1024)S(1)}, f32[2562]{0:T(1024)S(1)}, u32[]{:S(2)}, u32[]{:S(2)}) collective-permute-start(f32[2562]{0:T(1024)S(1)} %get-tuple-element.22), channel_id=1, source_target_pairs={{0,96},{8,104},{16,112},{24,120},{32,0},{40,8},{48,16},{56,24},{64... | collective-permute-start | bytes 30752 | tf_op jit(solution)/shard_map/ppermute | solution.py:47
  283.2 3.2 collective-permute-start.33
  324.2 4.0 %collective-permute-start.61 = (f32[40992]{0:T(1024)S(1)}, f32[40992]{0:T(1024)S(1)}, u32[]{:S(2)}, u32[]{:S(2)}) collective-permute-start(f32[40992]{0:T(1024)S(1)} %select_n.319), channel_id=1, source_target_pairs={{0,7},{1,0},{2,1},{3,2},{4,3},{5,4},{6,5},{7,6},{8,15},{9,8},{10,9... | collective-permute-start | bytes 491912 | tf_op jit(solution)/shard_map/ppermute | solution.py:36
  329.9 3.4 collective-permute-start.58
  336.2 5.0 %collective-permute-done.60 = f32[40992]{0:T(1024)S(1)} collective-permute-done((f32[40992]{0:T(1024)S(1)}, f32[40992]{0:T(1024)S(1)}, u32[]{:S(2)}, u32[]{:S(2)}) %collective-permute-start.60) | collective-permute-done | bytes 164000 | tf_op jit(solution)/shard_map/ppermute | solution.py:36
  346.5 3.8 %collective-permute-done.55 = f32[40992]{0:T(1024)S(1)} collective-permute-done((f32[40992]{0:T(1024)S(1)}, f32[40992]{0:T(1024)S(1)}, u32[]{:S(2)}, u32[]{:S(2)}) %collective-permute-start.55) | collective-permute-done | bytes 164000 | tf_op jit(solution)/shard_map/ppermute | solution.py:36
  350.4 6.3 %stack.187 = f32[8,40992]{1,0:T(8,128)S(1)} concatenate(f32[1,40992]{1,0:T(1,128)S(1)} %select_n.318, f32[1,40992]{1,0:T(1,128)S(1)} %stack.180, f32[1,40992]{1,0:T(1,128)S(1)} %stack.181, f32[1,40992]{1,0:T(1,128)S(1)} %stack.182, f32[1,40992]{1,0:T(1,128)S(1)} %stack.183, f32[1,40992]{1,0:T(1,128)S(1)} %stack.184, f32[1,40992]{1,0:T(1,128)S(1)} %stack.185, f32[1,40992]{1,0:T(1,128)S(1)} %stack.186), dimensions={0} | concatenate | bytes 2623488 | tf_op jit(solution)/shard_map/stack | solution.py:37
  (288 shorter events, 130.2 us)
Async XLA Ops:
  10.1 39.7 %collective-permute-start.2 = (bf16[3,1,1024,256]{3,2,1,0:T(8,128)(2,1)}, bf16[3,1,1024,256]{3,2,1,0:T(8,128)(2,1)}, u32[]{:S(2)}, u32[]{:S(2)}) collective-permute-start(bf16[3,1,1024,256]{3,2,1,0:T(8,128)(2,1)} %pad_maximum_fusion), channel_id=1, source_target_pairs={{0,1},{1,2},{2,3},{3,4},{4,5},{5,6},{6,7},{8,9},{9,10},{10,11},{11... | collective-permute-start | bytes 4718600 | tf_op jit(solution)/shard_map/ppermute | solution.py:26
  16.4 72.3 %collective-permute-start.3 = (bf16[3,1,1024,256]{3,2,1,0:T(8,128)(2,1)}, bf16[3,1,1024,256]{3,2,1,0:T(8,128)(2,1)}, u32[]{:S(2)}, u32[]{:S(2)}) collective-permute-start(bf16[3,1,1024,256]{3,2,1,0:T(8,128)(2,1)} %pad_maximum_fusion), channel_id=1, source_target_pairs={{1,0},{2,1},{3,2},{4,3},{5,4},{6,5},{7,6},{9,8},{10,9},{11,10},{12... | collective-permute-start | bytes 4718600 | tf_op jit(solution)/shard_map/ppermute | solution.py:27
  93.4 12.9 %collective-permute-start.4 = (bf16[512,256]{0,1:T(8,128)(2,1)S(1)}, bf16[512,256]{0,1:T(8,128)(2,1)S(1)}, u32[]{:S(2)}, u32[]{:S(2)}) collective-permute-start(bf16[512,256]{0,1:T(8,128)(2,1)S(1)} %get-tuple-element.35), channel_id=1, source_target_pairs={{0,1},{1,2},{2,3},{3,4},{4,5},{5,6},{6,7},{7,0},{8,9},{9,10},{10,1... | collective-permute-start | bytes 786440 | tf_op jit(solution)/shard_map/ppermute | solution.py:36
  93.6 14.7 %collective-permute-start.5 = (bf16[512,256]{0,1:T(8,128)(2,1)S(1)}, bf16[512,256]{0,1:T(8,128)(2,1)S(1)}, u32[]{:S(2)}, u32[]{:S(2)}) collective-permute-start(bf16[512,256]{0,1:T(8,128)(2,1)S(1)} %get-tuple-element.35), channel_id=1, source_target_pairs={{0,2},{1,3},{2,4},{3,5},{4,6},{5,7},{6,0},{7,1},{8,10},{9,11},{10,... | collective-permute-start | bytes 786440 | tf_op jit(solution)/shard_map/ppermute | solution.py:36
  96.1 30.6 %collective-permute-start.10 = (bf16[512,256]{0,1:T(8,128)(2,1)S(1)}, bf16[512,256]{0,1:T(8,128)(2,1)S(1)}, u32[]{:S(2)}, u32[]{:S(2)}) collective-permute-start(bf16[512,256]{0,1:T(8,128)(2,1)S(1)} %get-tuple-element.35), channel_id=1, source_target_pairs={{0,7},{1,0},{2,1},{3,2},{4,3},{5,4},{6,5},{7,6},{8,15},{9,8},{10,9... | collective-permute-start | bytes 786440 | tf_op jit(solution)/shard_map/ppermute | solution.py:36
  101.5 24.4 %collective-permute-start.9 = (bf16[512,256]{0,1:T(8,128)(2,1)S(1)}, bf16[512,256]{0,1:T(8,128)(2,1)S(1)}, u32[]{:S(2)}, u32[]{:S(2)}) collective-permute-start(bf16[512,256]{0,1:T(8,128)(2,1)S(1)} %get-tuple-element.35), channel_id=1, source_target_pairs={{0,6},{1,7},{2,0},{3,1},{4,2},{5,3},{6,4},{7,5},{8,14},{9,15},{10,... | collective-permute-start | bytes 786440 | tf_op jit(solution)/shard_map/ppermute | solution.py:36
  101.7 23.6 %collective-permute-start.8 = (bf16[512,256]{0,1:T(8,128)(2,1)S(1)}, bf16[512,256]{0,1:T(8,128)(2,1)S(1)}, u32[]{:S(2)}, u32[]{:S(2)}) collective-permute-start(bf16[512,256]{0,1:T(8,128)(2,1)S(1)} %get-tuple-element.35), channel_id=1, source_target_pairs={{0,5},{1,6},{2,7},{3,0},{4,1},{5,2},{6,3},{7,4},{8,13},{9,14},{10,... | collective-permute-start | bytes 786440 | tf_op jit(solution)/shard_map/ppermute | solution.py:36
  106.3 14.5 %collective-permute-start.6 = (bf16[512,256]{0,1:T(8,128)(2,1)S(1)}, bf16[512,256]{0,1:T(8,128)(2,1)S(1)}, u32[]{:S(2)}, u32[]{:S(2)}) collective-permute-start(bf16[512,256]{0,1:T(8,128)(2,1)S(1)} %get-tuple-element.35), channel_id=1, source_target_pairs={{0,3},{1,4},{2,5},{3,6},{4,7},{5,0},{6,1},{7,2},{8,11},{9,12},{10,... | collective-permute-start | bytes 786440 | tf_op jit(solution)/shard_map/ppermute | solution.py:36
  108.4 16.2 %collective-permute-start.7 = (bf16[512,256]{0,1:T(8,128)(2,1)S(1)}, bf16[512,256]{0,1:T(8,128)(2,1)S(1)}, u32[]{:S(2)}, u32[]{:S(2)}) collective-permute-start(bf16[512,256]{0,1:T(8,128)(2,1)S(1)} %get-tuple-element.35), channel_id=1, source_target_pairs={{0,4},{1,5},{2,6},{3,7},{4,0},{5,1},{6,2},{7,3},{8,12},{9,13},{10,... | collective-permute-start | bytes 786440 | tf_op jit(solution)/shard_map/ppermute | solution.py:36
  152.4 42.1 %collective-permute-start.12 = (bf16[512,256]{0,1:T(8,128)(2,1)}, bf16[512,256]{0,1:T(8,128)(2,1)}, u32[]{:S(2)}, u32[]{:S(2)}) collective-permute-start(bf16[512,256]{0,1:T(8,128)(2,1)} %get-tuple-element.46), channel_id=1, source_target_pairs={{0,2},{1,3},{2,4},{3,5},{4,6},{5,7},{6,0},{7,1},{8,10},{9,11},{10,... | collective-permute-start | bytes 786440 | tf_op jit(solution)/shard_map/ppermute | solution.py:36
  157.4 36.1 %collective-permute-start.11 = (bf16[512,256]{0,1:T(8,128)(2,1)}, bf16[512,256]{0,1:T(8,128)(2,1)}, u32[]{:S(2)}, u32[]{:S(2)}) collective-permute-start(bf16[512,256]{0,1:T(8,128)(2,1)} %get-tuple-element.46), channel_id=1, source_target_pairs={{0,1},{1,2},{2,3},{3,4},{4,5},{5,6},{6,7},{7,0},{8,9},{9,10},{10,1... | collective-permute-start | bytes 786440 | tf_op jit(solution)/shard_map/ppermute | solution.py:36
  183.4 25.6 %collective-permute-start.16 = (bf16[512,256]{0,1:T(8,128)(2,1)}, bf16[512,256]{0,1:T(8,128)(2,1)S(1)}, u32[]{:S(2)}, u32[]{:S(2)}) collective-permute-start(bf16[512,256]{0,1:T(8,128)(2,1)} %get-tuple-element.46), channel_id=1, source_target_pairs={{0,6},{1,7},{2,0},{3,1},{4,2},{5,3},{6,4},{7,5},{8,14},{9,15},{10,... | collective-permute-start | bytes 786440 | tf_op jit(solution)/shard_map/ppermute | solution.py:36
  186.6 20.3 %collective-permute-start.15 = (bf16[512,256]{0,1:T(8,128)(2,1)}, bf16[512,256]{0,1:T(8,128)(2,1)S(1)}, u32[]{:S(2)}, u32[]{:S(2)}) collective-permute-start(bf16[512,256]{0,1:T(8,128)(2,1)} %get-tuple-element.46), channel_id=1, source_target_pairs={{0,5},{1,6},{2,7},{3,0},{4,1},{5,2},{6,3},{7,4},{8,13},{9,14},{10,... | collective-permute-start | bytes 786440 | tf_op jit(solution)/shard_map/ppermute | solution.py:36
  190.3 16.6 %collective-permute-start.14 = (bf16[512,256]{0,1:T(8,128)(2,1)}, bf16[512,256]{0,1:T(8,128)(2,1)S(1)}, u32[]{:S(2)}, u32[]{:S(2)}) collective-permute-start(bf16[512,256]{0,1:T(8,128)(2,1)} %get-tuple-element.46), channel_id=1, source_target_pairs={{0,4},{1,5},{2,6},{3,7},{4,0},{5,1},{6,2},{7,3},{8,12},{9,13},{10,... | collective-permute-start | bytes 786440 | tf_op jit(solution)/shard_map/ppermute | solution.py:36
  193.5 13.4 %collective-permute-start.13 = (bf16[512,256]{0,1:T(8,128)(2,1)}, bf16[512,256]{0,1:T(8,128)(2,1)S(1)}, u32[]{:S(2)}, u32[]{:S(2)}) collective-permute-start(bf16[512,256]{0,1:T(8,128)(2,1)} %get-tuple-element.46), channel_id=1, source_target_pairs={{0,3},{1,4},{2,5},{3,6},{4,7},{5,0},{6,1},{7,2},{8,11},{9,12},{10,... | collective-permute-start | bytes 786440 | tf_op jit(solution)/shard_map/ppermute | solution.py:36
  194.5 14.5 %collective-permute-start.17 = (bf16[512,256]{0,1:T(8,128)(2,1)}, bf16[512,256]{0,1:T(8,128)(2,1)S(1)}, u32[]{:S(2)}, u32[]{:S(2)}) collective-permute-start(bf16[512,256]{0,1:T(8,128)(2,1)} %get-tuple-element.46), channel_id=1, source_target_pairs={{0,7},{1,0},{2,1},{3,2},{4,3},{5,4},{6,5},{7,6},{8,15},{9,8},{10,9... | collective-permute-start | bytes 786440 | tf_op jit(solution)/shard_map/ppermute | solution.py:36
  247.0 12.5 %collective-permute-start.18 = (f32[40992]{0:T(1024)S(1)}, f32[40992]{0:T(1024)S(1)}, u32[]{:S(2)}, u32[]{:S(2)}) collective-permute-start(f32[40992]{0:T(1024)S(1)} %get-tuple-element.7), channel_id=1, source_target_pairs={{0,1},{1,2},{2,3},{3,4},{4,5},{5,6},{6,7},{7,0},{8,9},{9,10},{10,1... | collective-permute-start | bytes 491912 | tf_op jit(solution)/shard_map/ppermute | solution.py:47
  249.4 10.6 %collective-permute-start.24 = (f32[40992]{0:T(1024)S(1)}, f32[40992]{0:T(1024)S(1)}, u32[]{:S(2)}, u32[]{:S(2)}) collective-permute-start(f32[40992]{0:T(1024)S(1)} %get-tuple-element.8), channel_id=1, source_target_pairs={{0,7},{1,0},{2,1},{3,2},{4,3},{5,4},{6,5},{7,6},{8,15},{9,8},{10,9... | collective-permute-start | bytes 491912 | tf_op jit(solution)/shard_map/ppermute | solution.py:47
  252.7 12.5 %collective-permute-start.23 = (f32[40992]{0:T(1024)S(1)}, f32[40992]{0:T(1024)S(1)}, u32[]{:S(2)}, u32[]{:S(2)}) collective-permute-start(f32[40992]{0:T(1024)S(1)} %get-tuple-element.9), channel_id=1, source_target_pairs={{0,6},{1,7},{2,0},{3,1},{4,2},{5,3},{6,4},{7,5},{8,14},{9,15},{10,... | collective-permute-start | bytes 491912 | tf_op jit(solution)/shard_map/ppermute | solution.py:47
  255.1 10.1 %collective-permute-start.22 = (f32[40992]{0:T(1024)S(1)}, f32[40992]{0:T(1024)S(1)}, u32[]{:S(2)}, u32[]{:S(2)}) collective-permute-start(f32[40992]{0:T(1024)S(1)} %get-tuple-element.10), channel_id=1, source_target_pairs={{0,5},{1,6},{2,7},{3,0},{4,1},{5,2},{6,3},{7,4},{8,13},{9,14},{10,... | collective-permute-start | bytes 491912 | tf_op jit(solution)/shard_map/ppermute | solution.py:47
  256.1 10.5 %collective-permute-start.21 = (f32[40992]{0:T(1024)S(1)}, f32[40992]{0:T(1024)S(1)}, u32[]{:S(2)}, u32[]{:S(2)}) collective-permute-start(f32[40992]{0:T(1024)S(1)} %get-tuple-element.11), channel_id=1, source_target_pairs={{0,4},{1,5},{2,6},{3,7},{4,0},{5,1},{6,2},{7,3},{8,12},{9,13},{10,... | collective-permute-start | bytes 491912 | tf_op jit(solution)/shard_map/ppermute | solution.py:47
  260.0 9.5 %collective-permute-start.19 = (f32[40992]{0:T(1024)S(1)}, f32[40992]{0:T(1024)S(1)}, u32[]{:S(2)}, u32[]{:S(2)}) collective-permute-start(f32[40992]{0:T(1024)S(1)} %get-tuple-element.13), channel_id=1, source_target_pairs={{0,2},{1,3},{2,4},{3,5},{4,6},{5,7},{6,0},{7,1},{8,10},{9,11},{10,... | collective-permute-start | bytes 491912 | tf_op jit(solution)/shard_map/ppermute | solution.py:47
  270.3 12.8 %collective-permute-start.25 = (f32[2562]{0:T(1024)S(1)}, f32[2562]{0:T(1024)S(1)}, u32[]{:S(2)}, u32[]{:S(2)}) collective-permute-start(f32[2562]{0:T(1024)S(1)} %get-tuple-element.18), channel_id=1, source_target_pairs={{0,8},{8,16},{16,24},{24,32},{32,40},{40,48},{48,56},{56,64},{64,7... | collective-permute-start | bytes 30752 | tf_op jit(solution)/shard_map/ppermute | solution.py:47
  270.4 12.8 %collective-permute-start.39 = (f32[2562]{0:T(1024)S(1)}, f32[2562]{0:T(1024)S(1)}, u32[]{:S(2)}, u32[]{:S(2)}) collective-permute-start(f32[2562]{0:T(1024)S(1)} %get-tuple-element.19), channel_id=1, source_target_pairs={{0,120},{8,0},{16,8},{24,16},{32,24},{40,32},{48,40},{56,48},{64,5... | collective-permute-start | bytes 30752 | tf_op jit(solution)/shard_map/ppermute | solution.py:47
  274.2 12.2 %collective-permute-start.37 = (f32[2562]{0:T(1024)S(1)}, f32[2562]{0:T(1024)S(1)}, u32[]{:S(2)}, u32[]{:S(2)}) collective-permute-start(f32[2562]{0:T(1024)S(1)} %get-tuple-element.21), channel_id=1, source_target_pairs={{0,104},{8,112},{16,120},{24,0},{32,8},{40,16},{48,24},{56,32},{64... | collective-permute-start | bytes 30752 | tf_op jit(solution)/shard_map/ppermute | solution.py:47
  274.7 12.0 %collective-permute-start.36 = (f32[2562]{0:T(1024)S(1)}, f32[2562]{0:T(1024)S(1)}, u32[]{:S(2)}, u32[]{:S(2)}) collective-permute-start(f32[2562]{0:T(1024)S(1)} %get-tuple-element.22), channel_id=1, source_target_pairs={{0,96},{8,104},{16,112},{24,120},{32,0},{40,8},{48,16},{56,24},{64... | collective-permute-start | bytes 30752 | tf_op jit(solution)/shard_map/ppermute | solution.py:47
  324.2 11.3 %collective-permute-start.61 = (f32[40992]{0:T(1024)S(1)}, f32[40992]{0:T(1024)S(1)}, u32[]{:S(2)}, u32[]{:S(2)}) collective-permute-start(f32[40992]{0:T(1024)S(1)} %select_n.319), channel_id=1, source_target_pairs={{0,7},{1,0},{2,1},{3,2},{4,3},{5,4},{6,5},{7,6},{8,15},{9,8},{10,9... | collective-permute-start | bytes 491912 | tf_op jit(solution)/shard_map/ppermute | solution.py:36
  328.2 13.1 %collective-permute-start.60 = (f32[40992]{0:T(1024)S(1)}, f32[40992]{0:T(1024)S(1)}, u32[]{:S(2)}, u32[]{:S(2)}) collective-permute-start(f32[40992]{0:T(1024)S(1)} %select_n.319), channel_id=1, source_target_pairs={{0,6},{1,7},{2,0},{3,1},{4,2},{5,3},{6,4},{7,5},{8,14},{9,15},{10,... | collective-permute-start | bytes 491912 | tf_op jit(solution)/shard_map/ppermute | solution.py:36
  329.7 15.3 %collective-permute-start.59 = (f32[40992]{0:T(1024)S(1)}, f32[40992]{0:T(1024)S(1)}, u32[]{:S(2)}, u32[]{:S(2)}) collective-permute-start(f32[40992]{0:T(1024)S(1)} %select_n.319), channel_id=1, source_target_pairs={{0,5},{1,6},{2,7},{3,0},{4,1},{5,2},{6,3},{7,4},{8,13},{9,14},{10,... | collective-permute-start | bytes 491912 | tf_op jit(solution)/shard_map/ppermute | solution.py:36
  329.9 15.3 %collective-permute-start.58 = (f32[40992]{0:T(1024)S(1)}, f32[40992]{0:T(1024)S(1)}, u32[]{:S(2)}, u32[]{:S(2)}) collective-permute-start(f32[40992]{0:T(1024)S(1)} %select_n.319), channel_id=1, source_target_pairs={{0,4},{1,5},{2,6},{3,7},{4,0},{5,1},{6,2},{7,3},{8,12},{9,13},{10,... | collective-permute-start | bytes 491912 | tf_op jit(solution)/shard_map/ppermute | solution.py:36
  333.3 12.0 %collective-permute-start.57 = (f32[40992]{0:T(1024)S(1)}, f32[40992]{0:T(1024)S(1)}, u32[]{:S(2)}, u32[]{:S(2)}) collective-permute-start(f32[40992]{0:T(1024)S(1)} %select_n.319), channel_id=1, source_target_pairs={{0,3},{1,4},{2,5},{3,6},{4,7},{5,0},{6,1},{7,2},{8,11},{9,12},{10,... | collective-permute-start | bytes 491912 | tf_op jit(solution)/shard_map/ppermute | solution.py:36
  335.6 10.8 %collective-permute-start.56 = (f32[40992]{0:T(1024)S(1)}, f32[40992]{0:T(1024)S(1)}, u32[]{:S(2)}, u32[]{:S(2)}) collective-permute-start(f32[40992]{0:T(1024)S(1)} %select_n.319), channel_id=1, source_target_pairs={{0,2},{1,3},{2,4},{3,5},{4,6},{5,7},{6,0},{7,1},{8,10},{9,11},{10,... | collective-permute-start | bytes 491912 | tf_op jit(solution)/shard_map/ppermute | solution.py:36
  (66 other events, 668.0 us)
